TPU v7x, 512 devices: a whole 4x8x8 slice. The times are simulated.
512 devices in a mesh: req: 64 (over x, y, core), tp: 8 (over z).
Axes of the slice: x: 4, y: 8, z: 8, core: 2. Of those that a mesh axis runs over, the one named last changes fastest.
Arguments:
- vit_context: bfloat16 [32768, 4096], P('req', 'tp'), may hold values from -6 to 6
- vision_residual: bfloat16 [32768, 4096], P('req', 'tp'), may hold values from -75 to 75
- out_weight: bfloat16 [4096, 4096], P('tp', 'req'), may hold values from -0.09375 to 0.09375
- layer_scale: float32 [4096], P('tp'), may hold values from 0.2 to 2
- prompt: bfloat16 [64, 256, 4096], P('req', None, 'tp'), may hold values from -75 to 75
- prompt_len: int32 [64], P('req'), may hold values from 128 to 256
- image_at: int32 [64], P('req'), may hold values from 0 to 128
- grid_sizes: int32 [128, 2], replicated, may hold values from 7 to 8, as said below
- image_owner: int32 [128], replicated, may hold values from 0 to 63, as said below
- norm_gain: float32 [4096], replicated, may hold values from 0.5 to 1.5
- qkv_weight: bfloat16 [4096, 6144], P('req', 'tp'), may hold values from -0.09375 to 0.09375
Outputs:
- qkv: bfloat16 [24576, 6144], P('req', 'tp')
Inputs may be any that keep to these rules, and one draw needn't show every extreme that they name: `image_owner`: each request owns exactly 2 images. `grid_sizes`: each side is 7 or 8; in every draw the images of some request are all 8 by 8, so that request has exactly 128 merged rows.
All inputs are finite; a program needn't handle non-finite values.
Results may differ from a plain program's by a relative error of at most 0.008.
Values may be sent and summed in bfloat16 or wider, within the bound.
No kernel may reach another device: no remote copies, remote signals or barrier semaphores. Data moves between devices by JAX's collectives and lax.ppermute only.
A program may use at most 64 MiB of HBM per device.

v0:
```python
import jax
import jax.numpy as jnp
from jax import lax
from jax.sharding import Mesh, PartitionSpec as P

HEAD = 128
GROUP = 4
IMG_MAX = 128
REQ = ("rx", "ry", "rc")


def request_plan(grid_sizes, image_owner, requests):
    image_rows = grid_sizes[:, 0] * grid_sizes[:, 1]
    member = (image_owner[:, None] == jnp.arange(requests, dtype=jnp.int32)[None, :]).astype(
        jnp.int32
    )
    counts = jnp.sum(image_rows[:, None] * member, axis=0)
    starts = jnp.cumsum(counts) - counts
    return (counts, starts)


def rope_tables(count):
    half_size = HEAD // 2
    exponent = jnp.arange(half_size, dtype=jnp.float32) * (2.0 / HEAD)
    frequency = jnp.exp(-exponent * jnp.log(jnp.float32(500000.0)))
    angles = jnp.arange(count, dtype=jnp.float32)[:, None] * frequency[None, :]
    return (jnp.cos(angles), jnp.sin(angles))


def apply_rope(projected, cosine_table, sine_table):
    seq_rows = projected.shape[0]
    head_blocks = projected.reshape(seq_rows, -1, GROUP + 2, HEAD)
    turning = head_blocks[:, :, : GROUP + 1, :]
    first_half = turning[..., : HEAD // 2]
    second_half = turning[..., HEAD // 2 :]
    cosine_wide = cosine_table[:, None, None, :]
    sine_wide = sine_table[:, None, None, :]
    turned = jnp.concatenate(
        [
            first_half * cosine_wide - second_half * sine_wide,
            second_half * cosine_wide + first_half * sine_wide,
        ],
        axis=-1,
    )
    head_blocks = jnp.concatenate([turned, head_blocks[:, :, GROUP + 1 :, :]], axis=2)
    return head_blocks.reshape(seq_rows, -1)


def normalize(embedded, norm_gain):
    values = embedded.astype(jnp.float32)
    mean_square = jnp.mean(values * values, axis=-1, keepdims=True)
    return (values * lax.rsqrt(mean_square + 1e-05) * norm_gain[None, :]).astype(jnp.bfloat16)


def gather_features(rows, tp_count):
    copies = jnp.broadcast_to(rows[None], (tp_count,) + rows.shape)
    blocks = lax.all_to_all(copies, "tp", 0, 0, tiled=True)
    return blocks.transpose(1, 0, 2).reshape(rows.shape[0], -1)


def shift(value, axis, step):
    size = lax.axis_size(axis)
    return lax.ppermute(value, axis, [(k, (k + step) % size) for k in range(size)])


def ring_gather(value, axis):
    size = lax.axis_size(axis)
    return jnp.stack([value] + [shift(value, axis, -step) for step in range(1, size)], axis=0)


def eight_gather(value, axis):
    from_next = shift(value, axis, -1)
    from_last = shift(value, axis, 1)
    three = jnp.stack([from_last, value, from_next], axis=0)
    far_next = shift(three, axis, -3)
    far_last = shift(three, axis, 3)
    return jnp.stack(
        [
            value,
            from_next,
            far_next[0],
            far_next[1],
            far_next[2],
            far_last[1],
            far_last[2],
            from_last,
        ],
        axis=0,
    )


def gather_plane(shard):
    by_y = eight_gather(shard, "ry") if lax.axis_size("ry") == 8 else ring_gather(shard, "ry")
    return ring_gather(by_y, "rx")


def shards(
    vit_context,
    vision_residual,
    out_weight,
    layer_scale,
    prompt,
    prompt_len,
    image_at,
    grid_sizes,
    image_owner,
    norm_gain,
    qkv_weight,
):
    requests = lax.axis_size(REQ)
    device_index = lax.axis_index(REQ)
    feature_width = vit_context.shape[1]
    merged_context = jnp.mean(
        vit_context.astype(jnp.float32).reshape(-1, 4, feature_width), axis=1
    ).astype(jnp.bfloat16)
    merged_residual = jnp.mean(
        vision_residual.astype(jnp.float32).reshape(-1, 4, feature_width), axis=1
    )
    swap = [(0, 1), (1, 0)]
    core = lax.axis_index("rc")
    context_pair = jnp.stack([merged_context, lax.ppermute(merged_context, "rc", swap)])
    context_ring = ring_gather(context_pair, "rx")
    weight_ring = (
        eight_gather(out_weight, "ry")
        if lax.axis_size("ry") == 8
        else ring_gather(out_weight, "ry")
    )
    parts = jnp.einsum(
        "dcgk,ykn->dcgyn", context_ring, weight_ring, preferred_element_type=jnp.float32
    ).astype(jnp.bfloat16)
    from_partner = lax.ppermute(parts[:, 1], "rc", swap)
    both = jnp.stack([parts[:, 0], from_partner], axis=-2)
    x_count = lax.axis_size("rx")
    landed = [both[0]] + [
        shift(both[(x_count - d) % x_count], "rx", (x_count - d) % x_count)
        for d in range(1, x_count)
    ]
    partial_value = jnp.moveaxis(jnp.stack(landed, axis=0), 0, 1)
    partial_value = jnp.where(core == 0, partial_value, partial_value[..., ::-1, :])
    partial_value = jnp.roll(partial_value, lax.axis_index("rx"), axis=1)
    partial_value = jnp.roll(partial_value, lax.axis_index("ry"), axis=2)
    own_part = merged_context
    partial_value = partial_value.reshape(own_part.shape[0], -1)
    tp_count = lax.axis_size("tp")
    block_terms = (
        partial_value.astype(jnp.bfloat16).reshape(-1, tp_count, feature_width).transpose(1, 0, 2)
    )
    own_share = jnp.sum(
        lax.all_to_all(block_terms, "tp", 0, 0, tiled=True).astype(jnp.float32), axis=0
    )
    merged = (merged_residual + layer_scale[None, :] * own_share).astype(jnp.bfloat16)
    merged_count = merged.shape[0]
    counts, starts = request_plan(grid_sizes, image_owner, requests)
    request_ends = starts + counts
    capacity = (IMG_MAX + requests - 1) // requests
    request_ids = jnp.arange(requests, dtype=jnp.int32)
    group_index = jnp.arange(merged_count, dtype=jnp.int32) * requests + device_index
    destination = jnp.sum((request_ends[None, :] <= group_index[:, None]).astype(jnp.int32), axis=1)
    owned_start = jnp.sum(
        jnp.where(destination[:, None] == request_ids[None, :], starts[None, :], 0), axis=1
    )
    target = destination * capacity + (group_index - owned_start) // requests
    usable = destination < requests
    send_slots = jnp.arange(requests * capacity, dtype=jnp.int32)
    placing = ((send_slots[:, None] == target[None, :]) & usable[None, :]).astype(jnp.bfloat16)
    outgoing = jnp.dot(placing, merged, preferred_element_type=jnp.float32).astype(jnp.bfloat16)
    arrived = lax.all_to_all(
        outgoing.reshape(requests, capacity, feature_width),
        REQ,
        split_axis=0,
        concat_axis=0,
        tiled=True,
    )
    arrived = arrived.reshape(requests * capacity, feature_width)
    own_request = request_ids == device_index
    own_count = jnp.sum(jnp.where(own_request, counts, 0))
    own_start = jnp.sum(jnp.where(own_request, starts, 0))
    image_from = image_at[0]
    prompt_count = prompt_len[0]
    seq_slots = prompt.shape[1] + IMG_MAX
    slot_index = jnp.arange(seq_slots, dtype=jnp.int32)
    image_row = slot_index - image_from
    in_image = (image_row >= 0) & (image_row < own_count)
    is_live = slot_index < prompt_count + own_count
    from_prompt = is_live & jnp.logical_not(in_image)
    prompt_row = jnp.where(slot_index < image_from, slot_index, slot_index - own_count)
    prompt_ids = jnp.arange(prompt.shape[1], dtype=jnp.int32)
    prompt_pick = ((prompt_row[:, None] == prompt_ids[None, :]) & from_prompt[:, None]).astype(
        jnp.bfloat16
    )
    full_image = gather_features(arrived, tp_count)
    full_prompt = lax.all_gather(prompt[0], "tp", axis=1, tiled=True)
    full_weight = lax.all_gather(qkv_weight, REQ, axis=0, tiled=True)
    cosine_table, sine_table = rope_tables(seq_slots)
    prompt_rows = jnp.dot(prompt_pick, full_prompt, preferred_element_type=jnp.float32)
    prompt_normed = normalize(prompt_rows.astype(jnp.bfloat16), norm_gain)
    prompt_out = apply_rope(
        jnp.dot(prompt_normed, full_weight, preferred_element_type=jnp.float32),
        cosine_table,
        sine_table,
    ).astype(jnp.bfloat16)
    image_ids = jnp.arange(IMG_MAX, dtype=jnp.int32)
    image_flat = (own_start + image_ids) % requests * capacity + image_ids // requests
    image_order = (
        (image_flat[:, None] == send_slots[None, :]) & (image_ids < own_count)[:, None]
    ).astype(jnp.bfloat16)
    full_image, prompt_out = lax.optimization_barrier((full_image, prompt_out))
    image_rows = jnp.dot(image_order, full_image, preferred_element_type=jnp.float32)
    image_normed = normalize(image_rows.astype(jnp.bfloat16), norm_gain)
    image_out = apply_rope(
        jnp.dot(image_normed, full_weight, preferred_element_type=jnp.float32),
        lax.dynamic_slice_in_dim(cosine_table, image_from, IMG_MAX, 0),
        lax.dynamic_slice_in_dim(sine_table, image_from, IMG_MAX, 0),
    ).astype(jnp.bfloat16)
    image_place = ((image_row[:, None] == image_ids[None, :]) & in_image[:, None]).astype(
        jnp.bfloat16
    )
    placed = jnp.dot(image_place, image_out, preferred_element_type=jnp.float32)
    return jnp.where(in_image[:, None], placed.astype(jnp.bfloat16), prompt_out)


def solution(mesh):
    in_specs = (
        P("req", "tp"),
        P("req", "tp"),
        P("tp", "req"),
        P("tp"),
        P("req", None, "tp"),
        P("req"),
        P("req"),
        P(),
        P(),
        P(),
        P("req", "tp"),
    )
    out_specs = P("req", "tp")
    rows, columns = mesh.devices.shape
    x_size = len({device.coords[0] for device in mesh.devices.flat})
    split_mesh = Mesh(mesh.devices.reshape(x_size, rows // (2 * x_size), 2, columns), REQ + ("tp",))
    rename = lambda spec: P(*(REQ if axis == "req" else axis for axis in spec))
    return jax.shard_map(
        shards,
        mesh=split_mesh,
        in_specs=tuple((rename(spec) for spec in in_specs)),
        out_specs=rename(out_specs),
        check_vma=False,
    )
```

profile of v0, /device:TPU:1, one launch (start us, length us, event | category | flops | bytes accessed | tf_op | source)
XLA Modules:
  0.0 181.3 jit_solution(1262390514091334798)
XLA Ops:
  6.5 0.7 all-gather.6.cloned.1.call-update
  7.3 0.7 all-gather.4.cloned.1.call-update
  8.0 5.9 %collective-permute-start.4 = (bf16[512,64]{0,1:T(8,128)(2,1)}, bf16[512,64]{0,1:T(8,128)(2,1)S(1)}, u32[]{:S(2)}, u32[]{:S(2)}) collective-permute-start(bf16[512,64]{0,1:T(8,128)(2,1)} %param.13), channel_id=1, source_target_pairs={{0,112},{16,0},{32,16},{48,32},{64,48},{80,64},{96,80},{112,96},{1... | collective-permute-start | bytes 196616 | tf_op jit(solution)/shard_map/ppermute | solution.py:63
  13.9 1.9 %collective-permute-start.5 = (bf16[512,64]{0,1:T(8,128)(2,1)}, bf16[512,64]{0,1:T(8,128)(2,1)S(1)}, u32[]{:S(2)}, u32[]{:S(2)}) collective-permute-start(bf16[512,64]{0,1:T(8,128)(2,1)} %param.13), channel_id=1, source_target_pairs={{0,16},{16,32},{32,48},{48,64},{64,80},{80,96},{96,112},{112,0},{1... | collective-permute-start | bytes 196616 | tf_op jit(solution)/shard_map/ppermute | solution.py:63
  15.9 1.4 reshape.242
  17.2 0.6 reduce_sum.96
  17.9 6.8 %collective-permute-start = (bf16[128,512]{1,0:T(8,128)(2,1)S(1)}, bf16[128,512]{1,0:T(8,128)(2,1)S(1)}, u32[]{:S(2)}, u32[]{:S(2)}) collective-permute-start(bf16[128,512]{1,0:T(8,128)(2,1)S(1)} %multiply_convert_fusion.2), channel_id=1, source_target_pairs={{0,8},{8,0},{1,9},{9,1},{2,10},{10,2},{3,11},{11,3},{4,12},{12,4},... | collective-permute-start | bytes 393224 | tf_op jit(solution)/shard_map/ppermute | solution.py:121
  24.8 1.9 %collective-permute-start.6 = (bf16[3,512,64]{1,2,0:T(8,128)(2,1)S(1)}, bf16[3,512,64]{1,2,0:T(8,128)(2,1)S(1)}, u32[]{:S(2)}, u32[]{:S(2)}) collective-permute-start(bf16[3,512,64]{1,2,0:T(8,128)(2,1)S(1)} %pad_maximum_fusion.3), channel_id=1, source_target_pairs={{0,80},{16,96},{32,112},{48,0},{64,16},{80,32},{96,48},{112,64},{1... | collective-permute-start | bytes 589832 | tf_op jit(solution)/shard_map/ppermute | solution.py:63
  26.7 5.2 %collective-permute-start.7 = (bf16[3,512,64]{1,2,0:T(8,128)(2,1)S(1)}, bf16[3,512,64]{1,2,0:T(8,128)(2,1)S(1)}, u32[]{:S(2)}, u32[]{:S(2)}) collective-permute-start(bf16[3,512,64]{1,2,0:T(8,128)(2,1)S(1)} %pad_maximum_fusion.3), channel_id=1, source_target_pairs={{0,48},{16,64},{32,80},{48,96},{64,112},{80,0},{96,16},{112,32},{1... | collective-permute-start | bytes 589832 | tf_op jit(solution)/shard_map/ppermute | solution.py:63
  32.0 1.9 %collective-permute-start.1 = (bf16[2,128,512]{2,1,0:T(8,128)(2,1)S(1)}, bf16[2,128,512]{2,1,0:T(8,128)(2,1)S(1)}, u32[]{:S(2)}, u32[]{:S(2)}) collective-permute-start(bf16[2,128,512]{2,1,0:T(8,128)(2,1)S(1)} %get-tuple-element.24), channel_id=1, source_target_pairs={{0,384},{128,0},{256,128},{384,256},{1,385},{129,1},{257,129},{385... | collective-permute-start | bytes 786440 | tf_op jit(solution)/shard_map/ppermute | solution.py:63
  33.9 1.9 %collective-permute-start.2 = (bf16[2,128,512]{2,1,0:T(8,128)(2,1)S(1)}, bf16[2,128,512]{2,1,0:T(8,128)(2,1)S(1)}, u32[]{:S(2)}, u32[]{:S(2)}) collective-permute-start(bf16[2,128,512]{2,1,0:T(8,128)(2,1)S(1)} %get-tuple-element.24), channel_id=1, source_target_pairs={{0,256},{128,384},{256,0},{384,128},{1,257},{129,385},{257,1},{385... | collective-permute-start | bytes 786440 | tf_op jit(solution)/shard_map/ppermute | solution.py:63
  35.8 3.4 %collective-permute-start.3 = (bf16[2,128,512]{2,1,0:T(8,128)(2,1)S(1)}, bf16[2,128,512]{2,1,0:T(8,128)(2,1)S(1)}, u32[]{:S(2)}, u32[]{:S(2)}) collective-permute-start(bf16[2,128,512]{2,1,0:T(8,128)(2,1)S(1)} %get-tuple-element.24), channel_id=1, source_target_pairs={{0,128},{128,256},{256,384},{384,0},{1,129},{129,257},{257,385},{3... | collective-permute-start | bytes 786440 | tf_op jit(solution)/shard_map/ppermute | solution.py:63
  39.2 7.2 %collective-permute-done.7 = bf16[3,512,64]{1,2,0:T(8,128)(2,1)S(1)} collective-permute-done((bf16[3,512,64]{1,2,0:T(8,128)(2,1)S(1)}, bf16[3,512,64]{1,2,0:T(8,128)(2,1)S(1)}, u32[]{:S(2)}, u32[]{:S(2)}) %collective-permute-start.7) | collective-permute-done | bytes 196640 | tf_op jit(solution)/shard_map/ppermute | solution.py:63
  46.5 4.8 %collective-permute-done.3 = bf16[2,128,512]{2,1,0:T(8,128)(2,1)S(1)} collective-permute-done((bf16[2,128,512]{2,1,0:T(8,128)(2,1)S(1)}, bf16[2,128,512]{2,1,0:T(8,128)(2,1)S(1)}, u32[]{:S(2)}, u32[]{:S(2)}) %collective-permute-start.3) | collective-permute-done | bytes 262176 | tf_op jit(solution)/shard_map/ppermute | solution.py:63
  51.2 0.7 convolution_convert_fusion.2
  52.1 2.3 %collective-permute-start.8 = (bf16[4,128,8,64]{1,3,2,0:T(8,128)(2,1)S(1)}, bf16[4,128,8,64]{1,3,2,0:T(8,128)(2,1)S(1)}, u32[]{:S(2)}, u32[]{:S(2)}) collective-permute-start(bf16[4,128,8,64]{1,3,2,0:T(8,128)(2,1)S(1)} %get-tuple-element.20), channel_id=1, source_target_pairs={{0,8},{8,0},{1,9},{9,1},{2,10},{10,2},{3,11},{11,3},{4,12},{12,4},... | collective-permute-start | bytes 1572872 | tf_op jit(solution)/shard_map/ppermute | solution.py:131
  54.4 1.5 collective-permute-done.8
  56.0 2.2 %collective-permute-start.9 = (bf16[128,8,2,64]{0,3,1,2:T(8,128)(2,1)S(1)}, bf16[128,8,2,64]{0,3,1,2:T(8,128)(2,1)S(1)}, u32[]{:S(2)}, u32[]{:S(2)}) collective-permute-start(bf16[128,8,2,64]{0,3,1,2:T(8,128)(2,1)S(1)} %get-tuple-element.16), channel_id=1, source_target_pairs={{0,384},{128,0},{256,128},{384,256},{1,385},{129,1},{257,129},{385... | collective-permute-start | bytes 786440 | tf_op jit(solution)/shard_map/ppermute | solution.py:63
  58.2 1.9 %collective-permute-start.10 = (bf16[128,8,2,64]{0,3,1,2:T(8,128)(2,1)S(1)}, bf16[128,8,2,64]{0,3,1,2:T(8,128)(2,1)S(1)}, u32[]{:S(2)}, u32[]{:S(2)}) collective-permute-start(bf16[128,8,2,64]{0,3,1,2:T(8,128)(2,1)S(1)} %get-tuple-element.18), channel_id=1, source_target_pairs={{0,256},{128,384},{256,0},{384,128},{1,257},{129,385},{257,1},{385... | collective-permute-start | bytes 786440 | tf_op jit(solution)/shard_map/ppermute | solution.py:63
  60.1 3.1 %collective-permute-start.11 = (bf16[128,8,2,64]{0,3,1,2:T(8,128)(2,1)S(1)}, bf16[128,8,2,64]{0,3,1,2:T(8,128)(2,1)S(1)}, u32[]{:S(2)}, u32[]{:S(2)}) collective-permute-start(bf16[128,8,2,64]{0,3,1,2:T(8,128)(2,1)S(1)} %get-tuple-element.17), channel_id=1, source_target_pairs={{0,128},{128,256},{256,384},{384,0},{1,129},{129,257},{257,385},{3... | collective-permute-start | bytes 786440 | tf_op jit(solution)/shard_map/ppermute | solution.py:63
  63.2 2.2 %collective-permute-done.9 = bf16[128,8,2,64]{0,3,1,2:T(8,128)(2,1)S(1)} collective-permute-done((bf16[128,8,2,64]{0,3,1,2:T(8,128)(2,1)S(1)}, bf16[128,8,2,64]{0,3,1,2:T(8,128)(2,1)S(1)}, u32[]{:S(2)}, u32[]{:S(2)}) %collective-permute-start.9) | collective-permute-done | bytes 262176 | tf_op jit(solution)/shard_map/ppermute | solution.py:63
  65.4 3.4 %collective-permute-done.10 = bf16[128,8,2,64]{0,3,1,2:T(8,128)(2,1)S(1)} collective-permute-done((bf16[128,8,2,64]{0,3,1,2:T(8,128)(2,1)S(1)}, bf16[128,8,2,64]{0,3,1,2:T(8,128)(2,1)S(1)}, u32[]{:S(2)}, u32[]{:S(2)}) %collective-permute-start.10) | collective-permute-done | bytes 262176 | tf_op jit(solution)/shard_map/ppermute | solution.py:63
  68.8 6.6 %collective-permute-done.11 = bf16[128,8,2,64]{0,3,1,2:T(8,128)(2,1)S(1)} collective-permute-done((bf16[128,8,2,64]{0,3,1,2:T(8,128)(2,1)S(1)}, bf16[128,8,2,64]{0,3,1,2:T(8,128)(2,1)S(1)}, u32[]{:S(2)}, u32[]{:S(2)}) %collective-permute-start.11) | collective-permute-done | bytes 262176 | tf_op jit(solution)/shard_map/ppermute | solution.py:63
  75.9 0.4 fusion.12
  76.3 0.4 fusion.11
  76.7 1.1 copy.43
  77.8 8.6 %all-to-all-start = ((bf16[8,128,512]{1,2,0:T(8,128)(2,1)}), bf16[8,128,512]{1,2,0:T(8,128)(2,1)S(1)}, u32[]{:S(2)}, u32[]{:S(2)}) async-start(bf16[8,128,512]{1,2,0:T(8,128)(2,1)} %bitcast.27), calls=%async_computation | async-start | bytes 2097152 | tf_op jit(solution)/shard_map/all_to_all | solution.py:149
  88.2 0.3 reshape.240
  88.5 0.6 reduce_sum.95
  89.2 0.7 fusion.52
  90.6 0.7 fusion.49
  91.3 0.7 subtract_select_fusion
  92.2 0.4 fusion.38
  92.6 23.0 %all-to-all-done = bf16[8,128,512]{1,2,0:T(8,128)(2,1)S(1)} async-done(((bf16[8,128,512]{1,2,0:T(8,128)(2,1)}), bf16[8,128,512]{1,2,0:T(8,128)(2,1)S(1)}, u32[]{:S(2)}, u32[]{:S(2)}) %all-to-all-start) | async-done | bytes 1048608 | tf_op jit(solution)/shard_map/all_to_all | solution.py:149
  116.1 0.7 reshape.235
  116.9 7.3 %all-to-all-start.1 = ((bf16[64,2,512]{2,1,0:T(2,128)(2,1)}), bf16[64,2,512]{2,1,0:T(2,128)(2,1)S(1)}, u32[]{:S(2)}, u32[]{:S(2)}) async-start(bf16[64,2,512]{2,1,0:T(2,128)(2,1)} %reshape.235), calls=%async_computation.1 | async-start | bytes 262144 | tf_op jit(solution)/shard_map/all_to_all | solution.py:167
  124.2 0.7 iota_compare_fusion.8
  125.0 9.8 %all-to-all-done.1 = bf16[64,2,512]{2,1,0:T(2,128)(2,1)S(1)} async-done(((bf16[64,2,512]{2,1,0:T(2,128)(2,1)}), bf16[64,2,512]{2,1,0:T(2,128)(2,1)S(1)}, u32[]{:S(2)}, u32[]{:S(2)}) %all-to-all-start.1) | async-done | bytes 131104 | tf_op jit(solution)/shard_map/all_to_all | solution.py:167
  134.9 1.1 broadcast_in_dim.28
  136.1 3.7 %all-to-all-start.2 = ((bf16[8,128,512]{1,2,0:T(8,128)(2,1)}), bf16[8,128,512]{1,2,0:T(8,128)(2,1)S(1)}, u32[]{:S(2)}, u32[]{:S(2)}) async-start(bf16[8,128,512]{1,2,0:T(8,128)(2,1)} %broadcast_in_dim.28), calls=%async_computation.2 | async-start | bytes 2097152 | tf_op jit(solution)/shard_map/all_to_all | solution.py:57
  139.8 0.6 fusion.50
  140.5 4.4 %fusion = (f32[384]{0:T(512)S(1)}, bf16[384,4096]{1,0:T(8,128)(2,1)}) fusion(bf16[1,256,4096]{2,1,0:T(8,128)(2,1)} %all-gather.6.cloned.1.call-done, s32[384]{0:T(512)S(1)} %subtract_select_fusion, pred[384]{0:T(512)(128)(4,1)S(1)} %get-tuple-element.11), kind=kOutput, calls=%fused_computation.2 | convolution fusion | flops 811794048 | bytes 5246336 | tf_op jit(solution)/shard_map/dot_general | solution.py:195
  144.9 4.5 %all-gather.4.cloned.1.call-done = bf16[4096,768]{1,0:T(8,128)(2,1)} async-done(((bf16[64,768]{1,0:T(8,128)(2,1)}), bf16[4096,768]{1,0:T(8,128)(2,1)}) %all-gather.4.cloned.1.call-update) | async-done | bytes 6291472 | tf_op jit(solution)/shard_map/all_gather | solution.py:193
  149.4 6.7 %fusion.4 = f32[384,768]{0,1:T(8,128)S(1)} fusion(bf16[4096,768]{1,0:T(8,128)(2,1)} %all-gather.4.cloned.1.call-done, bf16[384,4096]{1,0:T(8,128)(2,1)} %get-tuple-element.29, f32[4096]{0:T(1024)S(1)} %copy-done.2, f32[384]{0:T(512)S(1)} %add_rsqrt_fusion), kind=kOutput, calls=%fused_computation.8 | convolution fusion | flops 2422210560 | bytes 10634752 | tf_op jit(solution)/shard_map/dot_general | solution.py:198
  156.3 10.5 %all-to-all-done.2 = bf16[8,128,512]{1,2,0:T(8,128)(2,1)S(1)} async-done(((bf16[8,128,512]{1,2,0:T(8,128)(2,1)}), bf16[8,128,512]{1,2,0:T(8,128)(2,1)S(1)}, u32[]{:S(2)}, u32[]{:S(2)}) %all-to-all-start.2) | async-done | bytes 1048608 | tf_op jit(solution)/shard_map/all_to_all | solution.py:57
  166.9 0.6 multiply_reduce_fusion
  167.4 5.4 %fusion.10 = f32[128,768]{0,1:T(8,128)S(1)} fusion(bf16[4096,768]{1,0:T(8,128)(2,1)} %all-gather.4.cloned.1.call-done, f32[128,4096]{1,0:T(8,128)S(1)} %get-tuple-element.31, f32[4096]{0:T(1024)S(1)} %copy-done.2, f32[128]{0:T(128)S(1)} %add_rsqrt_fusion.1), kind=kOutput, calls=%fused_computation.30 | convolution fusion | flops 806879232 | bytes 8798720 | tf_op jit(solution)/shard_map/dot_general | solution.py:211
  173.2 1.2 fusion.9
  (61 shorter events, 2.8 us)
Async XLA Ops:
  6.5 18.2 %copy-start.1 = (bf16[512,64]{0,1:T(8,128)(2,1)S(1)}, bf16[512,64]{0,1:T(8,128)(2,1)}, u32[]{:S(2)}) copy-start(bf16[512,64]{0,1:T(8,128)(2,1)} %param.13) | copy-start | bytes 196612
  6.5 134.0 %all-gather.6.cloned.1.call-start = ((), (), s32[]{:S(2)}) async-start(), calls=%async_computation.4 | async-start | bytes 2359296 | tf_op jit(solution)/shard_map/all_gather | solution.py:192
  7.3 142.1 %all-gather.4.cloned.1.call-start = ((), (), s32[]{:S(2)}) async-start(), calls=%async_computation.3 | async-start | bytes 6389760 | tf_op jit(solution)/shard_map/all_gather | solution.py:193
  8.0 16.7 %collective-permute-start.4 = (bf16[512,64]{0,1:T(8,128)(2,1)}, bf16[512,64]{0,1:T(8,128)(2,1)S(1)}, u32[]{:S(2)}, u32[]{:S(2)}) collective-permute-start(bf16[512,64]{0,1:T(8,128)(2,1)} %param.13), channel_id=1, source_target_pairs={{0,112},{16,0},{32,16},{48,32},{64,48},{80,64},{96,80},{112,96},{1... | collective-permute-start | bytes 196616 | tf_op jit(solution)/shard_map/ppermute | solution.py:63
  13.9 10.8 %collective-permute-start.5 = (bf16[512,64]{0,1:T(8,128)(2,1)}, bf16[512,64]{0,1:T(8,128)(2,1)S(1)}, u32[]{:S(2)}, u32[]{:S(2)}) collective-permute-start(bf16[512,64]{0,1:T(8,128)(2,1)} %param.13), channel_id=1, source_target_pairs={{0,16},{16,32},{32,48},{48,64},{64,80},{80,96},{96,112},{112,0},{1... | collective-permute-start | bytes 196616 | tf_op jit(solution)/shard_map/ppermute | solution.py:63
  17.9 14.0 %collective-permute-start = (bf16[128,512]{1,0:T(8,128)(2,1)S(1)}, bf16[128,512]{1,0:T(8,128)(2,1)S(1)}, u32[]{:S(2)}, u32[]{:S(2)}) collective-permute-start(bf16[128,512]{1,0:T(8,128)(2,1)S(1)} %multiply_convert_fusion.2), channel_id=1, source_target_pairs={{0,8},{8,0},{1,9},{9,1},{2,10},{10,2},{3,11},{11,3},{4,12},{12,4},... | collective-permute-start | bytes 393224 | tf_op jit(solution)/shard_map/ppermute | solution.py:121
  24.8 14.4 %collective-permute-start.6 = (bf16[3,512,64]{1,2,0:T(8,128)(2,1)S(1)}, bf16[3,512,64]{1,2,0:T(8,128)(2,1)S(1)}, u32[]{:S(2)}, u32[]{:S(2)}) collective-permute-start(bf16[3,512,64]{1,2,0:T(8,128)(2,1)S(1)} %pad_maximum_fusion.3), channel_id=1, source_target_pairs={{0,80},{16,96},{32,112},{48,0},{64,16},{80,32},{96,48},{112,64},{1... | collective-permute-start | bytes 589832 | tf_op jit(solution)/shard_map/ppermute | solution.py:63
  26.7 19.7 %collective-permute-start.7 = (bf16[3,512,64]{1,2,0:T(8,128)(2,1)S(1)}, bf16[3,512,64]{1,2,0:T(8,128)(2,1)S(1)}, u32[]{:S(2)}, u32[]{:S(2)}) collective-permute-start(bf16[3,512,64]{1,2,0:T(8,128)(2,1)S(1)} %pad_maximum_fusion.3), channel_id=1, source_target_pairs={{0,48},{16,64},{32,80},{48,96},{64,112},{80,0},{96,16},{112,32},{1... | collective-permute-start | bytes 589832 | tf_op jit(solution)/shard_map/ppermute | solution.py:63
  32.0 14.5 %collective-permute-start.1 = (bf16[2,128,512]{2,1,0:T(8,128)(2,1)S(1)}, bf16[2,128,512]{2,1,0:T(8,128)(2,1)S(1)}, u32[]{:S(2)}, u32[]{:S(2)}) collective-permute-start(bf16[2,128,512]{2,1,0:T(8,128)(2,1)S(1)} %get-tuple-element.24), channel_id=1, source_target_pairs={{0,384},{128,0},{256,128},{384,256},{1,385},{129,1},{257,129},{385... | collective-permute-start | bytes 786440 | tf_op jit(solution)/shard_map/ppermute | solution.py:63
  33.9 12.6 %collective-permute-start.2 = (bf16[2,128,512]{2,1,0:T(8,128)(2,1)S(1)}, bf16[2,128,512]{2,1,0:T(8,128)(2,1)S(1)}, u32[]{:S(2)}, u32[]{:S(2)}) collective-permute-start(bf16[2,128,512]{2,1,0:T(8,128)(2,1)S(1)} %get-tuple-element.24), channel_id=1, source_target_pairs={{0,256},{128,384},{256,0},{384,128},{1,257},{129,385},{257,1},{385... | collective-permute-start | bytes 786440 | tf_op jit(solution)/shard_map/ppermute | solution.py:63
  35.8 15.4 %collective-permute-start.3 = (bf16[2,128,512]{2,1,0:T(8,128)(2,1)S(1)}, bf16[2,128,512]{2,1,0:T(8,128)(2,1)S(1)}, u32[]{:S(2)}, u32[]{:S(2)}) collective-permute-start(bf16[2,128,512]{2,1,0:T(8,128)(2,1)S(1)} %get-tuple-element.24), channel_id=1, source_target_pairs={{0,128},{128,256},{256,384},{384,0},{1,129},{129,257},{257,385},{3... | collective-permute-start | bytes 786440 | tf_op jit(solution)/shard_map/ppermute | solution.py:63
  52.1 3.8 %collective-permute-start.8 = (bf16[4,128,8,64]{1,3,2,0:T(8,128)(2,1)S(1)}, bf16[4,128,8,64]{1,3,2,0:T(8,128)(2,1)S(1)}, u32[]{:S(2)}, u32[]{:S(2)}) collective-permute-start(bf16[4,128,8,64]{1,3,2,0:T(8,128)(2,1)S(1)} %get-tuple-element.20), channel_id=1, source_target_pairs={{0,8},{8,0},{1,9},{9,1},{2,10},{10,2},{3,11},{11,3},{4,12},{12,4},... | collective-permute-start | bytes 1572872 | tf_op jit(solution)/shard_map/ppermute | solution.py:131
  56.0 9.4 %collective-permute-start.9 = (bf16[128,8,2,64]{0,3,1,2:T(8,128)(2,1)S(1)}, bf16[128,8,2,64]{0,3,1,2:T(8,128)(2,1)S(1)}, u32[]{:S(2)}, u32[]{:S(2)}) collective-permute-start(bf16[128,8,2,64]{0,3,1,2:T(8,128)(2,1)S(1)} %get-tuple-element.16), channel_id=1, source_target_pairs={{0,384},{128,0},{256,128},{384,256},{1,385},{129,1},{257,129},{385... | collective-permute-start | bytes 786440 | tf_op jit(solution)/shard_map/ppermute | solution.py:63
  58.2 10.6 %collective-permute-start.10 = (bf16[128,8,2,64]{0,3,1,2:T(8,128)(2,1)S(1)}, bf16[128,8,2,64]{0,3,1,2:T(8,128)(2,1)S(1)}, u32[]{:S(2)}, u32[]{:S(2)}) collective-permute-start(bf16[128,8,2,64]{0,3,1,2:T(8,128)(2,1)S(1)} %get-tuple-element.18), channel_id=1, source_target_pairs={{0,256},{128,384},{256,0},{384,128},{1,257},{129,385},{257,1},{385... | collective-permute-start | bytes 786440 | tf_op jit(solution)/shard_map/ppermute | solution.py:63
  60.1 15.3 %collective-permute-start.11 = (bf16[128,8,2,64]{0,3,1,2:T(8,128)(2,1)S(1)}, bf16[128,8,2,64]{0,3,1,2:T(8,128)(2,1)S(1)}, u32[]{:S(2)}, u32[]{:S(2)}) collective-permute-start(bf16[128,8,2,64]{0,3,1,2:T(8,128)(2,1)S(1)} %get-tuple-element.17), channel_id=1, source_target_pairs={{0,128},{128,256},{256,384},{384,0},{1,129},{129,257},{257,385},{3... | collective-permute-start | bytes 786440 | tf_op jit(solution)/shard_map/ppermute | solution.py:63
  76.7 9.8 %copy-start.4 = (s32[128,2]{0,1:T(2,128)S(1)}, s32[128,2]{0,1:T(2,128)}, u32[]{:S(2)}) copy-start(s32[128,2]{0,1:T(2,128)} %param.18) | copy-start | bytes 3076
  76.7 9.8 %copy-start.5 = (s32[128]{0:T(128)S(1)}, s32[128]{0:T(128)}, u32[]{:S(2)}) copy-start(s32[128]{0:T(128)} %param.19) | copy-start | bytes 1540
  76.7 11.5 %copy-start = (bf16[512,512]{1,0:T(8,128)(2,1)S(1)}, bf16[512,512]{1,0:T(8,128)(2,1)}, u32[]{:S(2)}) copy-start(bf16[512,512]{1,0:T(8,128)(2,1)} %param.12) | copy-start | bytes 1572868
  77.8 37.9 %all-to-all-start = ((bf16[8,128,512]{1,2,0:T(8,128)(2,1)}), bf16[8,128,512]{1,2,0:T(8,128)(2,1)S(1)}, u32[]{:S(2)}, u32[]{:S(2)}) async-start(bf16[8,128,512]{1,2,0:T(8,128)(2,1)} %bitcast.27), calls=%async_computation | async-start | bytes 2097152 | tf_op jit(solution)/shard_map/all_to_all | solution.py:149
  88.2 27.8 %copy-start.3 = (f32[512]{0:T(512)S(1)}, f32[512]{0:T(512)}, u32[]{:S(2)}) copy-start(f32[512]{0:T(512)} %param.14) | copy-start | bytes 6148
  116.9 17.9 %all-to-all-start.1 = ((bf16[64,2,512]{2,1,0:T(2,128)(2,1)}), bf16[64,2,512]{2,1,0:T(2,128)(2,1)S(1)}, u32[]{:S(2)}, u32[]{:S(2)}) async-start(bf16[64,2,512]{2,1,0:T(2,128)(2,1)} %reshape.235), calls=%async_computation.1 | async-start | bytes 262144 | tf_op jit(solution)/shard_map/all_to_all | solution.py:167
  136.1 30.8 %all-to-all-start.2 = ((bf16[8,128,512]{1,2,0:T(8,128)(2,1)}), bf16[8,128,512]{1,2,0:T(8,128)(2,1)S(1)}, u32[]{:S(2)}, u32[]{:S(2)}) async-start(bf16[8,128,512]{1,2,0:T(8,128)(2,1)} %broadcast_in_dim.28), calls=%async_computation.2 | async-start | bytes 2097152 | tf_op jit(solution)/shard_map/all_to_all | solution.py:57
  140.5 8.9 %copy-start.2 = (f32[4096]{0:T(1024)S(1)}, f32[4096]{0:T(1024)}, u32[]{:S(2)}) copy-start(f32[4096]{0:T(1024)} %param.20) | copy-start | bytes 49156
Sparse Core Ops, SparseCore 0:
  9.4 46.0 all-gather.5
  58.9 90.4 all-gather.3
where the time goes:
time: 182 us; the launch traced here: 181 us
  waiting for transfers between devices  74.9 us (41%)
  starting transfers between devices  58.1 us (32%)
  matrix products  19.2 us (11%)
  between operations  16 us (9%)
  other arithmetic  7.43 us (4%)
  local copies, waits for them, and re-layouts  5.56 us (3%)
    ppermute x10, starting transfers between devices, shift(): lax.ppermute(value, axis, [(k, (k + step) % size) for k in range(size)])  29.3 us
    ppermute x10, waiting for transfers between devices, shift(): lax.ppermute(value, axis, [(k, (k + step) % size) for k in range(size)])  24.2 us
    all_to_all x1, waiting for transfers between devices, shards(): lax.all_to_all(block_terms, 'tp', 0, 0, tiled=True).astype(jnp.float32)  23 us
    all_to_all x1, waiting for transfers between devices, gather_features(): blocks = lax.all_to_all(copies, 'tp', 0, 0, tiled=True)  10.5 us
    all_to_all x1, waiting for transfers between devices, shards(): lax.all_to_all(outgoing.reshape(requests, capacity, feature_width), REQ,...  9.79 us
    all_to_all x1, starting transfers between devices, shards(): lax.all_to_all(block_terms, 'tp', 0, 0, tiled=True).astype(jnp.float32)  8.64 us
    all_to_all x1, starting transfers between devices, shards(): lax.all_to_all(outgoing.reshape(requests, capacity, feature_width), REQ,...  7.3 us
    ppermute x1, starting transfers between devices, shards(): lax.ppermute(merged_context, 'rc', swap)  6.78 us
  transfers between devices with their start and end apart: 17, of which 10 were waited for; matrix products, arithmetic and copies ran while one was open for 14% of the time, Pallas kernels for 0%

commit v1 on v0

--- a/solution.py
+++ b/solution.py
@@ -190,7 +190,9 @@
     )
     full_image = gather_features(arrived, tp_count)
     full_prompt = lax.all_gather(prompt[0], "tp", axis=1, tiled=True)
-    full_weight = lax.all_gather(qkv_weight, REQ, axis=0, tiled=True)
+    full_weight = jnp.concatenate(
+        lax.all_to_all(jnp.stack([qkv_weight] * lax.axis_size(REQ)), REQ, 0, 0), axis=0
+    )
     cosine_table, sine_table = rope_tables(seq_slots)
     prompt_rows = jnp.dot(prompt_pick, full_prompt, preferred_element_type=jnp.float32)
     prompt_normed = normalize(prompt_rows.astype(jnp.bfloat16), norm_gain)

time: 182 us -> 329 us (1.81)
  waiting for transfers between devices: 74.9 us -> 190 us
  blocking collectives: 0 us -> 20.1 us
  local copies, waits for them, and re-layouts: 5.56 us -> 16.9 us
    all_to_all x1, waiting for transfers between devices: 9.79 us -> 135 us  [shards(): lax.all_to_all(jnp.stack([qkv_weight] * lax.axis_size(REQ)), REQ, 0, 0)]
    all_to_all x0 -> x1, blocking collectives: none -> 20.1 us  [shards(): lax.all_to_all(outgoing.reshape(requests, capacity, feature_width), REQ,...]
    dot_general x0 -> x1, local copies, waits for them, and re-layouts: none -> 8.64 us  [shards(): jnp.dot(prompt_normed, full_weight, preferred_element_type=jnp.float32)]
    ppermute x10, waiting for transfers between devices: 24.2 us -> 19.1 us  [shift(): lax.ppermute(value, axis, [(k, (k + step) % size) for k in range(size)])]
    all_gather x1 -> x0, waiting for transfers between devices: 4.49 us -> none  [shards(): full_weight = lax.all_gather(qkv_weight, REQ, axis=0, tiled=True)]
    all_to_all x1, waiting for transfers between devices: 10.5 us -> 6.59 us  [gather_features(): blocks = lax.all_to_all(copies, 'tp', 0, 0, tiled=True)]
    all_to_all x1, waiting for transfers between devices: 23 us -> 26.8 us  [shards(): lax.all_to_all(block_terms, 'tp', 0, 0, tiled=True).astype(jnp.float32)]
    another operation x1 -> x2, local copies, waits for them, and re-layouts: 0.1 us -> 3.51 us  [the longest x1 3.42 us: shards(): jnp.stack([qkv_weight] * lax.axis_size(REQ))]
  transfers between devices with their start and end apart: 17 -> 16, of which waited for: 10 -> 10; matrix products, arithmetic and copies ran while one was open for 14% -> 9% of each run, Pallas kernels for 0% -> 0%
where the time goes in v1:
time: 329 us; the launch traced here: 327 us
  waiting for transfers between devices  190 us (58%)
  starting transfers between devices  58.5 us (18%)
  blocking collectives  20.1 us (6%)
  matrix products  18.3 us (6%)
  local copies, waits for them, and re-layouts  16.9 us (5%)
  between operations  15.9 us (5%)
  other arithmetic  7.26 us (2%)
    all_to_all x1, waiting for transfers between devices, shards(): lax.all_to_all(jnp.stack([qkv_weight] * lax.axis_size(REQ)), REQ, 0, 0)  135 us
    ppermute x10, starting transfers between devices, shift(): lax.ppermute(value, axis, [(k, (k + step) % size) for k in range(size)])  32.7 us
    all_to_all x1, waiting for transfers between devices, shards(): lax.all_to_all(block_terms, 'tp', 0, 0, tiled=True).astype(jnp.float32)  26.8 us
    all_to_all x1, blocking collectives, shards(): lax.all_to_all(outgoing.reshape(requests, capacity, feature_width), REQ,...  20.1 us
    ppermute x10, waiting for transfers between devices, shift(): lax.ppermute(value, axis, [(k, (k + step) % size) for k in range(size)])  19.1 us
    dot_general x1, local copies, waits for them, and re-layouts, shards(): jnp.dot(prompt_normed, full_weight, preferred_element_type=jnp.float32)  8.64 us
    ppermute x1, starting transfers between devices, shards(): lax.ppermute(merged_context, 'rc', swap)  6.78 us
    dot_general x1, matrix products, shards(): jnp.dot(prompt_normed, full_weight, preferred_element_type=jnp.float32)  6.66 us
  transfers between devices with their start and end apart: 16, of which 10 were waited for; matrix products, arithmetic and copies ran while one was open for 9% of the time, Pallas kernels for 0%

profile of v1, /device:TPU:1, one launch (start us, length us, event | category | flops | bytes accessed | tf_op | source)
XLA Modules:
  0.0 326.7 jit_solution(461203441838020194)
XLA Ops:
  6.5 6.0 %collective-permute-start.4 = (bf16[512,64]{0,1:T(8,128)(2,1)}, bf16[512,64]{0,1:T(8,128)(2,1)S(1)}, u32[]{:S(2)}, u32[]{:S(2)}) collective-permute-start(bf16[512,64]{0,1:T(8,128)(2,1)} %param.13), channel_id=1, source_target_pairs={{0,112},{16,0},{32,16},{48,32},{64,48},{80,64},{96,80},{112,96},{1... | collective-permute-start | bytes 196616 | tf_op jit(solution)/shard_map/ppermute | solution.py:63
  12.6 1.9 collective-permute-start.5
  14.5 1.4 reshape.253
  15.9 0.6 reduce_sum.96
  16.5 6.8 %collective-permute-start = (bf16[128,512]{1,0:T(8,128)(2,1)S(1)}, bf16[128,512]{1,0:T(8,128)(2,1)S(1)}, u32[]{:S(2)}, u32[]{:S(2)}) collective-permute-start(bf16[128,512]{1,0:T(8,128)(2,1)S(1)} %multiply_convert_fusion.1), channel_id=1, source_target_pairs={{0,8},{8,0},{1,9},{9,1},{2,10},{10,2},{3,11},{11,3},{4,12},{12,4},... | collective-permute-start | bytes 393224 | tf_op jit(solution)/shard_map/ppermute | solution.py:121
  23.4 1.9 collective-permute-start.6
  25.4 5.2 %collective-permute-start.7 = (bf16[3,512,64]{1,2,0:T(8,128)(2,1)S(1)}, bf16[3,512,64]{1,2,0:T(8,128)(2,1)S(1)}, u32[]{:S(2)}, u32[]{:S(2)}) collective-permute-start(bf16[3,512,64]{1,2,0:T(8,128)(2,1)S(1)} %pad_maximum_fusion.3), channel_id=1, source_target_pairs={{0,48},{16,64},{32,80},{48,96},{64,112},{80,0},{96,16},{112,32},{1... | collective-permute-start | bytes 589832 | tf_op jit(solution)/shard_map/ppermute | solution.py:63
  30.6 1.9 collective-permute-start.3
  32.5 1.9 collective-permute-start.2
  34.5 4.6 %collective-permute-start.1 = (bf16[2,128,512]{2,1,0:T(8,128)(2,1)S(1)}, bf16[2,128,512]{2,1,0:T(8,128)(2,1)S(1)}, u32[]{:S(2)}, u32[]{:S(2)}) collective-permute-start(bf16[2,128,512]{2,1,0:T(8,128)(2,1)S(1)} %get-tuple-element.24), channel_id=1, source_target_pairs={{0,384},{128,0},{256,128},{384,256},{1,385},{129,1},{257,129},{385... | collective-permute-start | bytes 786440 | tf_op jit(solution)/shard_map/ppermute | solution.py:63
  39.1 6.0 %collective-permute-done.7 = bf16[3,512,64]{1,2,0:T(8,128)(2,1)S(1)} collective-permute-done((bf16[3,512,64]{1,2,0:T(8,128)(2,1)S(1)}, bf16[3,512,64]{1,2,0:T(8,128)(2,1)S(1)}, u32[]{:S(2)}, u32[]{:S(2)}) %collective-permute-start.7) | collective-permute-done | bytes 196640 | tf_op jit(solution)/shard_map/ppermute | solution.py:63
  45.1 1.5 collective-permute-done.3
  46.6 2.4 collective-permute-done.1
  49.0 0.7 convolution_convert_fusion.2
  49.9 3.5 %collective-permute-start.8 = (bf16[4,128,8,64]{1,3,2,0:T(8,128)(2,1)S(1)}, bf16[4,128,8,64]{1,3,2,0:T(8,128)(2,1)S(1)}, u32[]{:S(2)}, u32[]{:S(2)}) collective-permute-start(bf16[4,128,8,64]{1,3,2,0:T(8,128)(2,1)S(1)} %get-tuple-element.20), channel_id=1, source_target_pairs={{0,8},{8,0},{1,9},{9,1},{2,10},{10,2},{3,11},{11,3},{4,12},{12,4},... | collective-permute-start | bytes 1572872 | tf_op jit(solution)/shard_map/ppermute | solution.py:131
  53.3 1.5 collective-permute-done.8
  54.9 1.9 collective-permute-start.11
  56.9 5.4 %collective-permute-start.10 = (bf16[128,8,2,64]{0,3,1,2:T(8,128)(2,1)S(1)}, bf16[128,8,2,64]{0,3,1,2:T(8,128)(2,1)S(1)}, u32[]{:S(2)}, u32[]{:S(2)}) collective-permute-start(bf16[128,8,2,64]{0,3,1,2:T(8,128)(2,1)S(1)} %get-tuple-element.18), channel_id=1, source_target_pairs={{0,256},{128,384},{256,0},{384,128},{1,257},{129,385},{257,1},{385... | collective-permute-start | bytes 786440 | tf_op jit(solution)/shard_map/ppermute | solution.py:63
  62.3 1.9 collective-permute-start.9
  64.3 1.3 collective-permute-done.11
  65.6 6.5 %collective-permute-done.10 = bf16[128,8,2,64]{0,3,1,2:T(8,128)(2,1)S(1)} collective-permute-done((bf16[128,8,2,64]{0,3,1,2:T(8,128)(2,1)S(1)}, bf16[128,8,2,64]{0,3,1,2:T(8,128)(2,1)S(1)}, u32[]{:S(2)}, u32[]{:S(2)}) %collective-permute-start.10) | collective-permute-done | bytes 262176 | tf_op jit(solution)/shard_map/ppermute | solution.py:63
  72.0 1.4 collective-permute-done.9
  73.8 0.4 fusion.17
  74.2 0.4 fusion.16
  74.6 1.1 copy.43
  75.7 6.3 %all-to-all-start = ((bf16[8,128,512]{1,2,0:T(8,128)(2,1)}), bf16[8,128,512]{1,2,0:T(8,128)(2,1)S(1)}, u32[]{:S(2)}, u32[]{:S(2)}) async-start(bf16[8,128,512]{1,2,0:T(8,128)(2,1)} %bitcast.27), calls=%async_computation | async-start | bytes 2097152 | tf_op jit(solution)/shard_map/all_to_all | solution.py:149
  82.4 0.6 reduce_sum.95
  83.6 0.7 fusion.57
  84.3 26.8 %all-to-all-done = bf16[8,128,512]{1,2,0:T(8,128)(2,1)S(1)} async-done(((bf16[8,128,512]{1,2,0:T(8,128)(2,1)}), bf16[8,128,512]{1,2,0:T(8,128)(2,1)S(1)}, u32[]{:S(2)}, u32[]{:S(2)}) %all-to-all-start) | async-done | bytes 1048608 | tf_op jit(solution)/shard_map/all_to_all | solution.py:149
  111.7 20.1 %all_to_all.20 = bf16[64,2,512]{2,1,0:T(2,128)(2,1)S(1)} all-to-all(bf16[64,2,512]{2,1,0:T(2,128)(2,1)S(1)} %reshape.246), channel_id=1, replica_groups=mesh['rx'=4,'ry'=8,'rc'=2,'tp'=8] {'rx','ry','rc'}, dimensions={0} | all-to-all | bytes 262144 | tf_op jit(solution)/shard_map/all_to_all | solution.py:167
  131.9 3.4 %stack.57 = bf16[64,64,768]{2,1,0:T(8,128)(2,1)} broadcast(bf16[64,768]{1,0:T(8,128)(2,1)S(1)} %copy-done.2), dimensions={1,2} | broadcast | bytes 6389760 | tf_op jit(solution)/shard_map/stack | solution.py:194
  135.3 5.5 %all-to-all-start.3 = ((bf16[64,64,768]{2,1,0:T(8,128)(2,1)}), bf16[64,64,768]{2,1,0:T(8,128)(2,1)}, u32[]{:S(2)}, u32[]{:S(2)}) async-start(bf16[64,64,768]{2,1,0:T(8,128)(2,1)} %stack.57), calls=%async_computation.3 | async-start | bytes 12582912 | tf_op jit(solution)/shard_map/all_to_all | solution.py:194
  140.8 0.7 all-gather.3.cloned.1.call-update
  143.4 0.6 iota_compare_fusion.8
  144.1 0.7 fusion.55
  144.7 0.6 fusion.54
  145.4 0.6 subtract_select_fusion
  146.0 0.4 fusion.43
  146.7 134.9 %all-to-all-done.3 = bf16[64,64,768]{2,1,0:T(8,128)(2,1)} async-done(((bf16[64,64,768]{2,1,0:T(8,128)(2,1)}), bf16[64,64,768]{2,1,0:T(8,128)(2,1)}, u32[]{:S(2)}, u32[]{:S(2)}) %all-to-all-start.3) | async-done | bytes 6291488 | tf_op jit(solution)/shard_map/all_to_all | solution.py:194
  281.7 1.1 broadcast_in_dim.28
  282.8 3.7 %all-to-all-start.2 = ((bf16[8,128,512]{1,2,0:T(8,128)(2,1)}), bf16[8,128,512]{1,2,0:T(8,128)(2,1)S(1)}, u32[]{:S(2)}, u32[]{:S(2)}) async-start(bf16[8,128,512]{1,2,0:T(8,128)(2,1)} %broadcast_in_dim.28), calls=%async_computation.2 | async-start | bytes 2097152 | tf_op jit(solution)/shard_map/all_to_all | solution.py:57
  286.6 4.3 %fusion = (f32[384]{0:T(512)S(1)}, bf16[384,4096]{1,0:T(8,128)(2,1)}) fusion(bf16[1,256,4096]{2,1,0:T(8,128)(2,1)} %all-gather.3.cloned.1.call-done, s32[384]{0:T(512)S(1)} %subtract_select_fusion, pred[384]{0:T(512)(128)(4,1)S(1)} %get-tuple-element.11), kind=kOutput, calls=%fused_computation.2 | convolution fusion | flops 811794048 | bytes 5246336 | tf_op jit(solution)/shard_map/dot_general | solution.py:197
  290.9 8.6 %copy.46 = bf16[768,4096]{1,0:T(8,128)(2,1)} copy(bf16[768,4096]{0,1:T(8,128)(2,1)} %bitcast.34) | data formatting | bytes 12582912 | tf_op jit(solution)/shard_map/dot_general | solution.py:200
  299.5 6.7 %fusion.10 = f32[384,1,6,128]{0,3,2,1:T(8,128)S(1)} fusion(bf16[6,128,4096]{2,1,0:T(8,128)(2,1)} %bitcast.93, bf16[384,4096]{1,0:T(8,128)(2,1)} %get-tuple-element.29, f32[4096]{0:T(1024)S(1)} %copy-done.3, f32[384]{0:T(512)S(1)} %add_rsqrt_fusion), kind=kOutput, calls=%fused_computation.22 | convolution fusion | flops 2422210560 | bytes 10634752 | tf_op jit(solution)/shard_map/dot_general | solution.py:200
  306.4 6.6 %all-to-all-done.2 = bf16[8,128,512]{1,2,0:T(8,128)(2,1)S(1)} async-done(((bf16[8,128,512]{1,2,0:T(8,128)(2,1)}), bf16[8,128,512]{1,2,0:T(8,128)(2,1)S(1)}, u32[]{:S(2)}, u32[]{:S(2)}) %all-to-all-start.2) | async-done | bytes 1048608 | tf_op jit(solution)/shard_map/all_to_all | solution.py:57
  313.3 0.6 multiply_reduce_fusion
  313.8 4.7 %convolution_bitcast_fusion = f32[128,1,6,128]{0,3,2,1:T(8,128)S(1)} fusion(bf16[6,128,4096]{2,1,0:T(8,128)(2,1)} %bitcast.94, f32[128,4096]{1,0:T(8,128)S(1)} %get-tuple-element.31, f32[4096]{0:T(1024)S(1)} %copy-done.3, f32[128]{0:T(128)S(1)} %add_rsqrt_fusion.1), kind=kOutput, calls=%fused_computation.31 | convolution fusion | flops 806879232 | bytes 8798720 | tf_op jit(solution)/shard_map/dot_general | solution.py:213
  318.6 1.2 fusion.13
  (63 shorter events, 3.1 us)
Async XLA Ops:
  6.5 16.8 %copy-start.1 = (bf16[512,64]{0,1:T(8,128)(2,1)S(1)}, bf16[512,64]{0,1:T(8,128)(2,1)}, u32[]{:S(2)}) copy-start(bf16[512,64]{0,1:T(8,128)(2,1)} %param.13) | copy-start | bytes 196612
  6.5 16.9 %collective-permute-start.4 = (bf16[512,64]{0,1:T(8,128)(2,1)}, bf16[512,64]{0,1:T(8,128)(2,1)S(1)}, u32[]{:S(2)}, u32[]{:S(2)}) collective-permute-start(bf16[512,64]{0,1:T(8,128)(2,1)} %param.13), channel_id=1, source_target_pairs={{0,112},{16,0},{32,16},{48,32},{64,48},{80,64},{96,80},{112,96},{1... | collective-permute-start | bytes 196616 | tf_op jit(solution)/shard_map/ppermute | solution.py:63
  12.6 10.8 %collective-permute-start.5 = (bf16[512,64]{0,1:T(8,128)(2,1)}, bf16[512,64]{0,1:T(8,128)(2,1)S(1)}, u32[]{:S(2)}, u32[]{:S(2)}) collective-permute-start(bf16[512,64]{0,1:T(8,128)(2,1)} %param.13), channel_id=1, source_target_pairs={{0,16},{16,32},{32,48},{48,64},{64,80},{80,96},{96,112},{112,0},{1... | collective-permute-start | bytes 196616 | tf_op jit(solution)/shard_map/ppermute | solution.py:63
  16.5 14.0 %collective-permute-start = (bf16[128,512]{1,0:T(8,128)(2,1)S(1)}, bf16[128,512]{1,0:T(8,128)(2,1)S(1)}, u32[]{:S(2)}, u32[]{:S(2)}) collective-permute-start(bf16[128,512]{1,0:T(8,128)(2,1)S(1)} %multiply_convert_fusion.1), channel_id=1, source_target_pairs={{0,8},{8,0},{1,9},{9,1},{2,10},{10,2},{3,11},{11,3},{4,12},{12,4},... | collective-permute-start | bytes 393224 | tf_op jit(solution)/shard_map/ppermute | solution.py:121
  23.4 15.6 %collective-permute-start.6 = (bf16[3,512,64]{1,2,0:T(8,128)(2,1)S(1)}, bf16[3,512,64]{1,2,0:T(8,128)(2,1)S(1)}, u32[]{:S(2)}, u32[]{:S(2)}) collective-permute-start(bf16[3,512,64]{1,2,0:T(8,128)(2,1)S(1)} %pad_maximum_fusion.3), channel_id=1, source_target_pairs={{0,80},{16,96},{32,112},{48,0},{64,16},{80,32},{96,48},{112,64},{1... | collective-permute-start | bytes 589832 | tf_op jit(solution)/shard_map/ppermute | solution.py:63
  25.4 19.7 %collective-permute-start.7 = (bf16[3,512,64]{1,2,0:T(8,128)(2,1)S(1)}, bf16[3,512,64]{1,2,0:T(8,128)(2,1)S(1)}, u32[]{:S(2)}, u32[]{:S(2)}) collective-permute-start(bf16[3,512,64]{1,2,0:T(8,128)(2,1)S(1)} %pad_maximum_fusion.3), channel_id=1, source_target_pairs={{0,48},{16,64},{32,80},{48,96},{64,112},{80,0},{96,16},{112,32},{1... | collective-permute-start | bytes 589832 | tf_op jit(solution)/shard_map/ppermute | solution.py:63
  30.6 16.0 %collective-permute-start.3 = (bf16[2,128,512]{2,1,0:T(8,128)(2,1)S(1)}, bf16[2,128,512]{2,1,0:T(8,128)(2,1)S(1)}, u32[]{:S(2)}, u32[]{:S(2)}) collective-permute-start(bf16[2,128,512]{2,1,0:T(8,128)(2,1)S(1)} %get-tuple-element.24), channel_id=1, source_target_pairs={{0,128},{128,256},{256,384},{384,0},{1,129},{129,257},{257,385},{3... | collective-permute-start | bytes 786440 | tf_op jit(solution)/shard_map/ppermute | solution.py:63
  32.5 14.1 %collective-permute-start.2 = (bf16[2,128,512]{2,1,0:T(8,128)(2,1)S(1)}, bf16[2,128,512]{2,1,0:T(8,128)(2,1)S(1)}, u32[]{:S(2)}, u32[]{:S(2)}) collective-permute-start(bf16[2,128,512]{2,1,0:T(8,128)(2,1)S(1)} %get-tuple-element.24), channel_id=1, source_target_pairs={{0,256},{128,384},{256,0},{384,128},{1,257},{129,385},{257,1},{385... | collective-permute-start | bytes 786440 | tf_op jit(solution)/shard_map/ppermute | solution.py:63
  34.5 14.6 %collective-permute-start.1 = (bf16[2,128,512]{2,1,0:T(8,128)(2,1)S(1)}, bf16[2,128,512]{2,1,0:T(8,128)(2,1)S(1)}, u32[]{:S(2)}, u32[]{:S(2)}) collective-permute-start(bf16[2,128,512]{2,1,0:T(8,128)(2,1)S(1)} %get-tuple-element.24), channel_id=1, source_target_pairs={{0,384},{128,0},{256,128},{384,256},{1,385},{129,1},{257,129},{385... | collective-permute-start | bytes 786440 | tf_op jit(solution)/shard_map/ppermute | solution.py:63
  49.9 5.0 %collective-permute-start.8 = (bf16[4,128,8,64]{1,3,2,0:T(8,128)(2,1)S(1)}, bf16[4,128,8,64]{1,3,2,0:T(8,128)(2,1)S(1)}, u32[]{:S(2)}, u32[]{:S(2)}) collective-permute-start(bf16[4,128,8,64]{1,3,2,0:T(8,128)(2,1)S(1)} %get-tuple-element.20), channel_id=1, source_target_pairs={{0,8},{8,0},{1,9},{9,1},{2,10},{10,2},{3,11},{11,3},{4,12},{12,4},... | collective-permute-start | bytes 1572872 | tf_op jit(solution)/shard_map/ppermute | solution.py:131
  54.9 10.6 %collective-permute-start.11 = (bf16[128,8,2,64]{0,3,1,2:T(8,128)(2,1)S(1)}, bf16[128,8,2,64]{0,3,1,2:T(8,128)(2,1)S(1)}, u32[]{:S(2)}, u32[]{:S(2)}) collective-permute-start(bf16[128,8,2,64]{0,3,1,2:T(8,128)(2,1)S(1)} %get-tuple-element.17), channel_id=1, source_target_pairs={{0,128},{128,256},{256,384},{384,0},{1,129},{129,257},{257,385},{3... | collective-permute-start | bytes 786440 | tf_op jit(solution)/shard_map/ppermute | solution.py:63
  56.9 15.2 %collective-permute-start.10 = (bf16[128,8,2,64]{0,3,1,2:T(8,128)(2,1)S(1)}, bf16[128,8,2,64]{0,3,1,2:T(8,128)(2,1)S(1)}, u32[]{:S(2)}, u32[]{:S(2)}) collective-permute-start(bf16[128,8,2,64]{0,3,1,2:T(8,128)(2,1)S(1)} %get-tuple-element.18), channel_id=1, source_target_pairs={{0,256},{128,384},{256,0},{384,128},{1,257},{129,385},{257,1},{385... | collective-permute-start | bytes 786440 | tf_op jit(solution)/shard_map/ppermute | solution.py:63
  62.3 11.1 %collective-permute-start.9 = (bf16[128,8,2,64]{0,3,1,2:T(8,128)(2,1)S(1)}, bf16[128,8,2,64]{0,3,1,2:T(8,128)(2,1)S(1)}, u32[]{:S(2)}, u32[]{:S(2)}) collective-permute-start(bf16[128,8,2,64]{0,3,1,2:T(8,128)(2,1)S(1)} %get-tuple-element.16), channel_id=1, source_target_pairs={{0,384},{128,0},{256,128},{384,256},{1,385},{129,1},{257,129},{385... | collective-permute-start | bytes 786440 | tf_op jit(solution)/shard_map/ppermute | solution.py:63
  74.6 7.4 %copy-start = (bf16[512,512]{1,0:T(8,128)(2,1)S(1)}, bf16[512,512]{1,0:T(8,128)(2,1)}, u32[]{:S(2)}) copy-start(bf16[512,512]{1,0:T(8,128)(2,1)} %param.12) | copy-start | bytes 1572868
  75.7 7.3 %copy-start.5 = (s32[128,2]{0,1:T(2,128)S(1)}, s32[128,2]{0,1:T(2,128)}, u32[]{:S(2)}) copy-start(s32[128,2]{0,1:T(2,128)} %param.18) | copy-start | bytes 3076
  75.7 7.3 %copy-start.6 = (s32[128]{0:T(128)S(1)}, s32[128]{0:T(128)}, u32[]{:S(2)}) copy-start(s32[128]{0:T(128)} %param.19) | copy-start | bytes 1540
  75.7 35.5 %all-to-all-start = ((bf16[8,128,512]{1,2,0:T(8,128)(2,1)}), bf16[8,128,512]{1,2,0:T(8,128)(2,1)S(1)}, u32[]{:S(2)}, u32[]{:S(2)}) async-start(bf16[8,128,512]{1,2,0:T(8,128)(2,1)} %bitcast.27), calls=%async_computation | async-start | bytes 2097152 | tf_op jit(solution)/shard_map/all_to_all | solution.py:149
  82.0 29.5 %copy-start.4 = (f32[512]{0:T(512)S(1)}, f32[512]{0:T(512)}, u32[]{:S(2)}) copy-start(f32[512]{0:T(512)} %param.14) | copy-start | bytes 6148
  82.3 49.5 %copy-start.2 = (bf16[64,768]{1,0:T(8,128)(2,1)S(1)}, bf16[64,768]{1,0:T(8,128)(2,1)}, u32[]{:S(2)}) copy-start(bf16[64,768]{1,0:T(8,128)(2,1)} %param.21) | copy-start | bytes 294916
  135.3 146.4 %all-to-all-start.3 = ((bf16[64,64,768]{2,1,0:T(8,128)(2,1)}), bf16[64,64,768]{2,1,0:T(8,128)(2,1)}, u32[]{:S(2)}, u32[]{:S(2)}) async-start(bf16[64,64,768]{2,1,0:T(8,128)(2,1)} %stack.57), calls=%async_computation.3 | async-start | bytes 12582912 | tf_op jit(solution)/shard_map/all_to_all | solution.py:194
  140.8 145.8 %all-gather.3.cloned.1.call-start = ((), (), s32[]{:S(2)}) async-start(), calls=%async_computation.4 | async-start | bytes 2359296 | tf_op jit(solution)/shard_map/all_gather | solution.py:192
  282.8 30.2 %all-to-all-start.2 = ((bf16[8,128,512]{1,2,0:T(8,128)(2,1)}), bf16[8,128,512]{1,2,0:T(8,128)(2,1)S(1)}, u32[]{:S(2)}, u32[]{:S(2)}) async-start(bf16[8,128,512]{1,2,0:T(8,128)(2,1)} %broadcast_in_dim.28), calls=%async_computation.2 | async-start | bytes 2097152 | tf_op jit(solution)/shard_map/all_to_all | solution.py:57
  290.9 8.6 %copy-start.3 = (f32[4096]{0:T(1024)S(1)}, f32[4096]{0:T(1024)}, u32[]{:S(2)}) copy-start(f32[4096]{0:T(1024)} %param.20) | copy-start | bytes 49156
Sparse Core Ops, SparseCore 0:
  143.7 36.4 all-gather.2
